TPU v7x, 256 devices: a whole 4x4x8 slice. The times are simulated.
256 devices in a mesh: tm: 64 (over y, z, core), state: 4 (over x).
Axes of the slice: x: 4, y: 4, z: 8, core: 2. Of those that a mesh axis runs over, the one named last changes fastest.
Arguments:
- dynamics: float32 [512, 512], P('state'), may hold values from -1 to 1
- pattern: int32 [4, 4], replicated, may hold values from 0 to 1
- initial_mean: float32 [4, 512], replicated, may hold values from -6 to 6
- observed: float32 [1024, 4], P('tm'), may hold values from -6 to 6
- obs_index: int32 [1024], P('tm'), may hold values from 0 to 511
- obs_noise: float32 [1024], P('tm'), may hold values from 0.5 to 4
Outputs:
- filtered: float32 [1024, 4, 512], P('tm', 'state')
- smoothed: float32 [1024, 4, 512], P('tm', 'state')
All inputs are finite; a program needn't handle non-finite values.
Results may differ from a plain program's by a relative error of at most 0.0003.
Values sent between devices are 32-bit elements; how exact they have to be, the bound alone decides.
No kernel may reach another device: no remote copies, remote signals or barrier semaphores. Data moves between devices by JAX's collectives and lax.ppermute only.
A program may use at most 256 MiB of HBM per device.

v0:
```python
import jax
import jax.numpy as jnp
from jax import lax
from jax.sharding import PartitionSpec as P


def passed_along(block, axis, distance):
    devices = range(lax.axis_size(axis))
    route = [(i - distance, i) for i in devices if i - distance in devices]
    return lax.ppermute(block, axis, route)


def product(left, right):
    return jnp.dot(left, right, precision=lax.Precision.HIGHEST, preferred_element_type=jnp.float32)


def transposed(left, right):
    return lax.dot_general(
        left,
        right,
        (((1,), (1,)), ((), ())),
        precision=lax.Precision.HIGHEST,
        preferred_element_type=jnp.float32,
    )


def select_tree(usable, first_tree, second_tree):

    def select_leaf(first_leaf, second_leaf):
        return jnp.where(usable, first_leaf, second_leaf)

    return jax.tree.map(select_leaf, first_tree, second_tree)


def per_device(dynamics, pattern, initial_mean, observed, obs_index, obs_noise):
    row_count = dynamics.shape[0]
    state_width = dynamics.shape[1]
    blocks = pattern.shape[0]
    block_span = state_width // blocks
    seq_total = initial_mean.shape[0]
    steps_here = observed.shape[0]
    members = lax.axis_size("state")
    member = lax.axis_index("state")
    segments = lax.axis_size("tm")
    segment = lax.axis_index("tm")
    batch_here = seq_total // members
    present = jnp.maximum(pattern, jnp.eye(blocks, dtype=jnp.int32))
    block_mask = jnp.repeat(jnp.repeat(present, block_span, 0), block_span, 1).astype(jnp.float32)
    transition = lax.all_gather(dynamics, "state", axis=0, tiled=True) * block_mask
    kalman_gains = 1.0 / (1.0 + obs_noise)
    state_index = jnp.arange(state_width, dtype=jnp.int32)
    observed_masks = (state_index[None, :] == obs_index[:, None]).astype(jnp.float32)
    scale_factors = 1.0 - kalman_gains[:, None] * observed_masks
    final_local = jnp.arange(steps_here, dtype=jnp.int32) == steps_here - 1
    retain_flags = 1.0 - jnp.where((segment == segments - 1) & final_local, 1.0, 0.0).astype(
        jnp.float32
    )
    first_row = member * row_count
    owned_rows = (
        jnp.arange(row_count, dtype=jnp.int32)[:, None] + first_row == state_index[None, :]
    ).astype(jnp.float32)
    batch_start = member * batch_here
    local_observations = lax.dynamic_slice_in_dim(observed, batch_start, batch_here, 1)

    def combine_rows(earlier_full, later):
        return (
            product(later[0], earlier_full[0]),
            transposed(earlier_full[1], later[0]) + later[1],
        )

    def doubling(element, direction):
        identity = (owned_rows, jnp.zeros((seq_total, row_count), jnp.float32))
        distances = [1]
        for level_turn in range(9):
            if 2**level_turn < segments:
                distances.append(2**level_turn)
        current = element
        for level_turn, distance in enumerate(distances):
            arrived = passed_along(current, "tm", direction * distance)
            if direction > 0:
                usable = segment >= distance
            else:
                usable = segment + distance < segments
            if level_turn == 0:
                current = select_tree(usable, arrived, identity)
            else:
                gathered = (
                    lax.all_gather(arrived[0], "state", axis=0, tiled=True),
                    lax.all_gather(arrived[1], "state", axis=1, tiled=True),
                )
                current = select_tree(usable, combine_rows(gathered, current), current)
        return current

    def entering(element, start_mean, direction):
        map_rows, map_offsets = doubling(element, direction)
        if start_mean is None:
            entry_rows = map_offsets
        else:
            entry_rows = map_offsets + transposed(start_mean, map_rows)
        return lax.all_to_all(entry_rows, "state", split_axis=0, concat_axis=1, tiled=True)

    def filter_portion(carried, inputs):
        row_block, offsets = carried
        hit_mask, scaling, gain_now, obs_now = inputs
        column_now = product(row_block, hit_mask)
        offsets = offsets + gain_now * obs_now[:, None] * column_now[None, :]
        row_block = product(row_block * scaling[None, :], transition)
        return ((row_block, offsets), None)

    initial_shifts = jnp.zeros((seq_total, row_count), jnp.float32)
    (filter_rows, filter_offsets), unused_value = lax.scan(
        filter_portion,
        (owned_rows, initial_shifts),
        (observed_masks, scale_factors, kalman_gains, observed),
        reverse=True,
    )
    filter_input = entering((filter_rows, filter_offsets), initial_mean, 1)

    def forward_sweep(current_state, inputs):
        scaling, hit_mask, gain_now, obs_now = inputs
        current_state = (
            transposed(current_state, transition) * scaling[None, :]
            + gain_now * obs_now[:, None] * hit_mask[None, :]
        )
        return (current_state, current_state)

    unused_value, filtered = lax.scan(
        forward_sweep,
        filter_input,
        (scale_factors, observed_masks, kalman_gains, local_observations),
    )
    flat_means = filtered.reshape(steps_here * batch_here, state_width)
    backward_mapped = product(transposed(flat_means, transition), transition).reshape(
        steps_here, batch_here, state_width
    )
    residual_terms = (
        filtered - retain_flags[:, None, None] * backward_mapped * scale_factors[:, None, :]
    )

    def smoother_update(current_state, inputs):
        scaling, keep_flag, gap_term = inputs
        current_state = keep_flag * product(current_state, transition) * scaling[None, :] + gap_term
        return (current_state, current_state)

    zero_portion = jnp.zeros((batch_here, state_width), jnp.float32)
    local_shifts, unused_value = lax.scan(
        smoother_update, zero_portion, (scale_factors, retain_flags, residual_terms), reverse=True
    )
    smooth_offsets = lax.all_to_all(local_shifts, "state", split_axis=1, concat_axis=0, tiled=True)

    def smoother_portion(row_block, inputs):
        scaling, keep_flag = inputs
        return (keep_flag * transposed(row_block * scaling[None, :], transition), None)

    smoother_rows, unused_value = lax.scan(
        smoother_portion, owned_rows, (scale_factors, retain_flags)
    )
    smoother_input = entering((smoother_rows, smooth_offsets), None, -1)
    unused_value, smoothed = lax.scan(
        smoother_update, smoother_input, (scale_factors, retain_flags, residual_terms), reverse=True
    )
    return (filtered, smoothed)


def solution(mesh):
    return jax.shard_map(
        per_device,
        mesh=mesh,
        in_specs=(P("state", None), P(), P(), P("tm", None), P("tm"), P("tm")),
        out_specs=(P("tm", "state", None), P("tm", "state", None)),
        check_vma=False,
    )
```

profile of v0, /device:TPU:8, one launch (start us, length us, event | category | flops | bytes accessed | tf_op | source)
XLA Modules:
  0.0 767.9 jit_solution(12369168793150731097)
XLA Ops:
  10.4 29.0 %all-gather.13.cloned.1.call-done = f32[512,512]{1,0:T(8,128)} async-done(((f32[128,512]{1,0:T(8,128)}), f32[512,512]{1,0:T(8,128)}) %all-gather.13.cloned.1.call-update) | async-done | bytes 1048592 | tf_op jit(solution)/shard_map/all_gather | solution.py:49
  40.8 40.3 %while.71 = (s32[]{:T(128)}, f32[128,512]{1,0:T(8,128)S(1)}, f32[16]{0:T(128)S(1)}, f32[16,512]{1,0:T(8,128)S(1)}, f32[512,512]{1,0:T(8,128)S(1)}, /*index=5*/s32[]{:T(128)}) while((s32[]{:T(128)}, f32[128,512]{1,0:T(8,128)S(1)}, f32[16]{0:T(128)S(1)}, f32[16,512]{1,0:T(8,128)S(1)}, f32[512,512]{1,0:T(8,128)S(1)}, /*index=5*/s32[]{:T(128)}) %tuple.143), condition=%wide.region_7.8_spmd, body=%wide.region_6.7_spmd.sunk | while | flops 402784256 | bytes 2103393 | solution.py:155
  81.1 2.6 collective-permute-start.16
  83.7 38.8 %while.73 = (s32[]{:T(128)}, f32[128,512]{1,0:T(8,128)S(1)}, f32[4,128]{1,0:T(4,128)S(1)}, f32[16,512]{1,0:T(8,128)S(1)}, f32[512,512]{1,0:T(8,128)S(1)}, /*inde...) while((s32[]{:T(128)}, f32[128,512]{1,0:T(8,128)S(1)}, ...), condition=%wide.region_1.2_spmd.clone, body=%wide.region_0.1_spmd.clone.sunk | while | flops 403506688 | bytes 2372823 | solution.py:111
  124.4 7.9 %collective-permute-done.2 = f32[128,512]{1,0:T(8,128)S(1)} collective-permute-done((f32[128,512]{1,0:T(8,128)S(1)}, f32[128,512]{1,0:T(8,128)S(1)}, u32[]{:S(2)}, u32[]{:S(2)}) %collective-permute-start.2) | collective-permute-done | bytes 262176 | tf_op jit(solution)/shard_map/ppermute | solution.py:10
  134.3 7.9 %collective-permute-done.4 = f32[128,512]{1,0:T(8,128)S(1)} collective-permute-done((f32[128,512]{1,0:T(8,128)S(1)}, f32[128,512]{1,0:T(8,128)S(1)}, u32[]{:S(2)}, u32[]{:S(2)}) %collective-permute-start.4) | collective-permute-done | bytes 262176 | tf_op jit(solution)/shard_map/ppermute | solution.py:10
  142.9 24.7 %all-gather.15.cloned.1.call-done = f32[512,512]{1,0:T(8,128)} async-done(((f32[128,512]{1,0:T(8,128)}), f32[512,512]{1,0:T(8,128)}) %all-gather.15.cloned.1.call-update) | async-done | bytes 1048592 | tf_op jit(solution)/shard_map/all_gather | solution.py:88
  169.5 3.5 collective-permute-start.6
  173.0 6.9 collective-permute-done.6
  182.6 3.9 collective-permute-done.18
  187.3 19.8 %all-gather.17.cloned.1.call-done = f32[512,512]{1,0:T(8,128)} async-done(((f32[128,512]{1,0:T(8,128)}), f32[512,512]{1,0:T(8,128)}) %all-gather.17.cloned.1.call-update) | async-done | bytes 1048592 | tf_op jit(solution)/shard_map/all_gather | solution.py:88
  209.0 4.5 collective-permute-start.8
  213.5 9.2 %collective-permute-done.8 = f32[128,512]{1,0:T(8,128)S(1)} collective-permute-done((f32[128,512]{1,0:T(8,128)S(1)}, f32[128,512]{1,0:T(8,128)S(1)}, u32[]{:S(2)}, u32[]{:S(2)}) %collective-permute-start.8) | collective-permute-done | bytes 262176 | tf_op jit(solution)/shard_map/ppermute | solution.py:10
  223.5 12.3 %all-gather.27.cloned.1.call-done = f32[512,512]{1,0:T(8,128)} async-done(((f32[128,512]{1,0:T(8,128)}), f32[512,512]{1,0:T(8,128)}) %all-gather.27.cloned.1.call-update) | async-done | bytes 1048592 | tf_op jit(solution)/shard_map/all_gather | solution.py:88
  237.7 5.2 collective-permute-start.20
  242.9 3.9 collective-permute-done.20
  247.6 16.9 %all-gather.19.cloned.1.call-done = f32[512,512]{1,0:T(8,128)} async-done(((f32[128,512]{1,0:T(8,128)}), f32[512,512]{1,0:T(8,128)}) %all-gather.19.cloned.1.call-update) | async-done | bytes 1048592 | tf_op jit(solution)/shard_map/all_gather | solution.py:88
  266.4 7.6 collective-permute-start.10
  274.1 7.1 collective-permute-done.10
  282.0 11.2 %all-gather.29.cloned.1.call-done = f32[512,512]{1,0:T(8,128)} async-done(((f32[128,512]{1,0:T(8,128)}), f32[512,512]{1,0:T(8,128)}) %all-gather.29.cloned.1.call-update) | async-done | bytes 1048592 | tf_op jit(solution)/shard_map/all_gather | solution.py:88
  295.1 6.0 collective-permute-start.22
  301.2 9.1 %collective-permute-done.22 = f32[128,512]{1,0:T(8,128)S(1)} collective-permute-done((f32[128,512]{1,0:T(8,128)S(1)}, f32[128,512]{1,0:T(8,128)S(1)}, u32[]{:S(2)}, u32[]{:S(2)}) %collective-permute-start.22) | collective-permute-done | bytes 262176 | tf_op jit(solution)/shard_map/ppermute | solution.py:10
  311.1 11.0 %all-gather.21.cloned.1.call-done = f32[512,512]{1,0:T(8,128)} async-done(((f32[128,512]{1,0:T(8,128)}), f32[512,512]{1,0:T(8,128)}) %all-gather.21.cloned.1.call-update) | async-done | bytes 1048592 | tf_op jit(solution)/shard_map/all_gather | solution.py:88
  324.0 3.4 collective-permute-start.12
  327.4 4.9 collective-permute-done.12
  333.1 17.9 %all-gather.31.cloned.1.call-done = f32[512,512]{1,0:T(8,128)} async-done(((f32[128,512]{1,0:T(8,128)}), f32[512,512]{1,0:T(8,128)}) %all-gather.31.cloned.1.call-update) | async-done | bytes 1048592 | tf_op jit(solution)/shard_map/all_gather | solution.py:88
  352.9 7.6 collective-permute-start.24
  360.5 9.2 %collective-permute-done.24 = f32[128,512]{1,0:T(8,128)} collective-permute-done((f32[128,512]{1,0:T(8,128)S(1)}, f32[128,512]{1,0:T(8,128)}, u32[]{:S(2)}, u32[]{:S(2)}) %collective-permute-start.24) | collective-permute-done | bytes 262176 | tf_op jit(solution)/shard_map/ppermute | solution.py:10
  369.8 10.0 %all-gather.23.cloned.1.call-done = f32[512,512]{1,0:T(8,128)} async-done(((f32[128,512]{1,0:T(8,128)}), f32[512,512]{1,0:T(8,128)}) %all-gather.23.cloned.1.call-update) | async-done | bytes 1048592 | tf_op jit(solution)/shard_map/all_gather | solution.py:88
  382.4 4.7 collective-permute-start.13
  390.3 3.8 collective-permute-done
  396.1 5.1 collective-permute-done.1
  401.2 10.4 %all_gather.73 = f32[4,512]{1,0:T(4,128)S(1)} all-gather(f32[4,128]{1,0:T(4,128)S(1)} %collective-permute-done.1), channel_id=1, replica_groups=mesh['tm'=64,'state'=4] {'state'}, dimensions={1}, use_global_device_ids=true | all-gather | bytes 10240 | tf_op jit(solution)/shard_map/all_gather | solution.py:89
  413.8 5.7 collective-permute-done.3
  419.5 10.6 %all_gather.74 = f32[4,512]{1,0:T(4,128)S(1)} all-gather(f32[4,128]{1,0:T(4,128)S(1)} %collective-permute-done.3), channel_id=1, replica_groups=mesh['tm'=64,'state'=4] {'state'}, dimensions={1}, use_global_device_ids=true | all-gather | bytes 10240 | tf_op jit(solution)/shard_map/all_gather | solution.py:89
  432.3 6.6 collective-permute-done.5
  438.9 10.5 %all_gather.76 = f32[4,512]{1,0:T(4,128)S(1)} all-gather(f32[4,128]{1,0:T(4,128)S(1)} %collective-permute-done.5), channel_id=1, replica_groups=mesh['tm'=64,'state'=4] {'state'}, dimensions={1}, use_global_device_ids=true | all-gather | bytes 10240 | tf_op jit(solution)/shard_map/all_gather | solution.py:89
  449.6 4.2 collective-permute-start.7
  453.8 6.2 collective-permute-done.7
  460.0 10.5 %all_gather.78 = f32[4,512]{1,0:T(4,128)S(1)} all-gather(f32[4,128]{1,0:T(4,128)S(1)} %collective-permute-done.7), channel_id=1, replica_groups=mesh['tm'=64,'state'=4] {'state'}, dimensions={1}, use_global_device_ids=true | all-gather | bytes 10240 | tf_op jit(solution)/shard_map/all_gather | solution.py:89
  472.7 3.5 collective-permute-done.9
  476.2 10.7 %all_gather.80 = f32[4,512]{1,0:T(4,128)S(1)} all-gather(f32[4,128]{1,0:T(4,128)S(1)} %collective-permute-done.9), channel_id=1, replica_groups=mesh['tm'=64,'state'=4] {'state'}, dimensions={1}, use_global_device_ids=true | all-gather | bytes 10240 | tf_op jit(solution)/shard_map/all_gather | solution.py:89
  487.2 2.5 collective-permute-start.11
  491.7 3.6 collective-permute-start.26
  495.3 10.5 %all_gather.82 = f32[4,512]{1,0:T(4,128)S(1)} all-gather(f32[4,128]{1,0:T(4,128)S(1)} %collective-permute-done.11), channel_id=1, replica_groups=mesh['tm'=64,'state'=4] {'state'}, dimensions={1}, use_global_device_ids=true | all-gather | bytes 10240 | tf_op jit(solution)/shard_map/all_gather | solution.py:89
  509.0 3.7 all-to-all-start
  513.4 4.5 all-to-all-done
  517.9 55.4 %while.70 = (s32[]{:T(128)}, f32[1,512]{1,0:T(1,128)S(1)}, f32[16,1,512]{2,1,0:T(1,128)S(1)}, f32[512,512]{1,0:T(8,128)S(1)}, f32[16,512]{1,0:T(8,128)S(1)}, /*i...) while((s32[]{:T(128)}, f32[1,512]{1,0:T(1,128)S(1)}, ...), condition=%wide.region_3.4_spmd, body=%wide.region_2.3_spmd.sunk | while | flops 3147267 | bytes 1063049 | solution.py:127
  574.9 30.2 %while.74 = (s32[]{:T(128)}, f32[1,512]{1,0:T(1,128)S(1)}, f32[16]{0:T(128)S(1)}, f32[512,512]{1,0:T(8,128)S(1)}, f32[16,512]{1,0:T(8,128)S(1)}, /*index=5*/f32[...) while((s32[]{:T(128)}, f32[1,512]{1,0:T(1,128)S(1)}, f32[16]{0:T(128)S(1)}, ...), condition=%wide.region_5.6_spmd.clone, body=%wide.region_4.5_spmd.clone.sunk | while | flops 3147780 | bytes 1065103 | solution.py:146
  605.1 7.6 all_to_all.48
  616.0 5.7 collective-permute-start.15
  623.0 10.4 %all_gather.85 = f32[4,512]{1,0:T(4,128)S(1)} all-gather(f32[4,128]{1,0:T(4,128)S(1)} %collective-permute-done.15), channel_id=1, replica_groups=mesh['tm'=64,'state'=4] {'state'}, dimensions={1}, use_global_device_ids=true | all-gather | bytes 10240 | tf_op jit(solution)/shard_map/all_gather | solution.py:89
  635.6 3.6 collective-permute-done.17
  639.2 10.6 %all_gather.86 = f32[4,512]{1,0:T(4,128)S(1)} all-gather(f32[4,128]{1,0:T(4,128)S(1)} %collective-permute-done.17), channel_id=1, replica_groups=mesh['tm'=64,'state'=4] {'state'}, dimensions={1}, use_global_device_ids=true | all-gather | bytes 10240 | tf_op jit(solution)/shard_map/all_gather | solution.py:89
  652.0 4.4 collective-permute-done.19
  656.5 10.4 %all_gather.88 = f32[4,512]{1,0:T(4,128)S(1)} all-gather(f32[4,128]{1,0:T(4,128)S(1)} %collective-permute-done.19), channel_id=1, replica_groups=mesh['tm'=64,'state'=4] {'state'}, dimensions={1}, use_global_device_ids=true | all-gather | bytes 10240 | tf_op jit(solution)/shard_map/all_gather | solution.py:89
  669.1 7.5 collective-permute-done.21
  676.6 10.6 %all_gather.90 = f32[4,512]{1,0:T(4,128)S(1)} all-gather(f32[4,128]{1,0:T(4,128)S(1)} %collective-permute-done.21), channel_id=1, replica_groups=mesh['tm'=64,'state'=4] {'state'}, dimensions={1}, use_global_device_ids=true | all-gather | bytes 10240 | tf_op jit(solution)/shard_map/all_gather | solution.py:89
  689.4 3.5 collective-permute-done.23
  692.9 10.4 %all_gather.92 = f32[4,512]{1,0:T(4,128)S(1)} all-gather(f32[4,128]{1,0:T(4,128)S(1)} %collective-permute-done.23), channel_id=1, replica_groups=mesh['tm'=64,'state'=4] {'state'}, dimensions={1}, use_global_device_ids=true | all-gather | bytes 10240 | tf_op jit(solution)/shard_map/all_gather | solution.py:89
  707.0 3.7 collective-permute-done.25
  710.7 10.6 %all_gather.94 = f32[4,512]{1,0:T(4,128)S(1)} all-gather(f32[4,128]{1,0:T(4,128)S(1)} %collective-permute-done.25), channel_id=1, replica_groups=mesh['tm'=64,'state'=4] {'state'}, dimensions={1}, use_global_device_ids=true | all-gather | bytes 10240 | tf_op jit(solution)/shard_map/all_gather | solution.py:89
  721.5 8.7 %all_to_all.49 = f32[4,1,128]{2,1,0:T(1,128)S(1)} all-to-all(f32[4,1,128]{2,1,0:T(1,128)S(1)} %bitcast.189), channel_id=1, replica_groups=mesh['tm'=64,'state'=4] {'state'}, dimensions={0} | all-to-all | bytes 4096 | tf_op jit(solution)/shard_map/all_to_all | solution.py:100
  730.2 30.3 %while.72 = (s32[]{:T(128)}, f32[1,512]{1,0:T(1,128)S(1)}, f32[16,1,512]{2,1,0:T(1,128)S(1)}, f32[16]{0:T(128)S(1)}, f32[512,512]{1,0:T(8,128)S(1)}, /*index=5*/...) while((s32[]{:T(128)}, f32[1,512]{1,0:T(1,128)S(1)}, f32[16,1,512]{2,1,0:T(1,128)S(1)}, ...), condition=%wide.region_9.10_spmd, body=%wide.region_8.9_spmd.sunk | while | flops 3147267 | bytes 1067141 | solution.py:159
  (500 shorter events, 262.9 us)
Async XLA Ops:
  7.2 500.6 %copy-start = (f32[4,512]{1,0:T(4,128)S(1)}, f32[4,512]{1,0:T(4,128)}, u32[]{:S(2)}) copy-start(f32[4,512]{1,0:T(4,128)} %param.18) | copy-start | bytes 24580
  7.2 32.2 %all-gather.13.cloned.1.call-start = ((), (), s32[]{:S(2)}) async-start(), calls=%async_computation.3 | async-start | bytes 1310720 | tf_op jit(solution)/shard_map/all_gather | solution.py:49
  7.9 159.7 %all-gather.15.cloned.1.call-start = ((), (), s32[]{:S(2)}) async-start(), calls=%async_computation.4 | async-start | bytes 1310720 | tf_op jit(solution)/shard_map/all_gather | solution.py:88
  8.1 0.7 copy-start.16
  8.8 0.7 copy-start.18
  8.9 0.7 copy-start.17
  9.6 0.7 copy-start.15
  39.3 1.2 copy-start.3
  81.1 43.2 %collective-permute-start.16 = (f32[128,512]{1,0:T(8,128)S(1)}, f32[128,512]{1,0:T(8,128)S(1)}, u32[]{:S(2)}, u32[]{:S(2)}) collective-permute-start(f32[128,512]{1,0:T(8,128)S(1)} %get-tuple-element.499), channel_id=1, source_target_pairs={{4,0},{8,4},{12,8},{16,12},{20,16},{24,20},{28,24},{32,28},{36,32}... | collective-permute-start | bytes 786440 | tf_op jit(solution)/shard_map/ppermute | solution.py:10
  122.4 9.8 %collective-permute-start.2 = (f32[128,512]{1,0:T(8,128)S(1)}, f32[128,512]{1,0:T(8,128)S(1)}, u32[]{:S(2)}, u32[]{:S(2)}) collective-permute-start(f32[128,512]{1,0:T(8,128)S(1)} %get-tuple-element.496), channel_id=1, source_target_pairs={{0,4},{4,8},{8,12},{12,16},{16,20},{20,24},{24,28},{28,32},{32,36}... | collective-permute-start | bytes 786440 | tf_op jit(solution)/shard_map/ppermute | solution.py:10
  132.3 9.8 %collective-permute-start.4 = (f32[128,512]{1,0:T(8,128)S(1)}, f32[128,512]{1,0:T(8,128)S(1)}, u32[]{:S(2)}, u32[]{:S(2)}) collective-permute-start(f32[128,512]{1,0:T(8,128)S(1)} %get-tuple-element.664), channel_id=1, source_target_pairs={{0,4},{4,8},{8,12},{12,16},{16,20},{20,24},{24,28},{28,32},{32,36}... | collective-permute-start | bytes 786440 | tf_op jit(solution)/shard_map/ppermute | solution.py:10
  142.1 0.7 copy-start.13
  142.9 64.2 %all-gather.17.cloned.1.call-start = ((), (), s32[]{:S(2)}) async-start(), calls=%async_computation.5 | async-start | bytes 1310720 | tf_op jit(solution)/shard_map/all_gather | solution.py:88
  169.5 10.4 %collective-permute-start.6 = (f32[128,512]{1,0:T(8,128)S(1)}, f32[128,512]{1,0:T(8,128)S(1)}, u32[]{:S(2)}, u32[]{:S(2)}) collective-permute-start(f32[128,512]{1,0:T(8,128)S(1)} %convolution_select_fusion.10), channel_id=1, source_target_pairs={{0,8},{4,12},{8,16},{12,20},{16,24},{20,28},{24,32},{28,36},{32,40... | collective-permute-start | bytes 786440 | tf_op jit(solution)/shard_map/ppermute | solution.py:10
  179.9 0.7 copy-start.12
  180.7 55.1 %all-gather.27.cloned.1.call-start = ((), (), s32[]{:S(2)}) async-start(), calls=%async_computation.10 | async-start | bytes 1310720 | tf_op jit(solution)/shard_map/all_gather | solution.py:88
  180.7 5.8 collective-permute-start.18
  186.5 0.7 copy-start.10
  187.2 77.2 %all-gather.19.cloned.1.call-start = ((), (), s32[]{:S(2)}) async-start(), calls=%async_computation.6 | async-start | bytes 1310720 | tf_op jit(solution)/shard_map/all_gather | solution.py:88
  209.0 13.7 %collective-permute-start.8 = (f32[128,512]{1,0:T(8,128)S(1)}, f32[128,512]{1,0:T(8,128)S(1)}, u32[]{:S(2)}, u32[]{:S(2)}) collective-permute-start(f32[128,512]{1,0:T(8,128)S(1)} %convolution_select_fusion.9), channel_id=1, source_target_pairs={{0,16},{4,20},{8,24},{12,28},{16,32},{20,36},{24,40},{28,44},{32,4... | collective-permute-start | bytes 786440 | tf_op jit(solution)/shard_map/ppermute | solution.py:10
  222.7 0.7 copy-start.11
  223.4 69.7 %all-gather.29.cloned.1.call-start = ((), (), s32[]{:S(2)}) async-start(), calls=%async_computation.11 | async-start | bytes 1310720 | tf_op jit(solution)/shard_map/all_gather | solution.py:88
  237.7 9.1 %collective-permute-start.20 = (f32[128,512]{1,0:T(8,128)S(1)}, f32[128,512]{1,0:T(8,128)S(1)}, u32[]{:S(2)}, u32[]{:S(2)}) collective-permute-start(f32[128,512]{1,0:T(8,128)S(1)} %convolution_select_fusion.4), channel_id=1, source_target_pairs={{8,0},{12,4},{16,8},{20,12},{24,16},{28,20},{32,24},{36,28},{40,32... | collective-permute-start | bytes 786440 | tf_op jit(solution)/shard_map/ppermute | solution.py:10
  246.8 0.7 copy-start.6
  247.5 74.5 %all-gather.21.cloned.1.call-start = ((), (), s32[]{:S(2)}) async-start(), calls=%async_computation.7 | async-start | bytes 1310720 | tf_op jit(solution)/shard_map/all_gather | solution.py:88
  266.4 14.8 %collective-permute-start.10 = (f32[128,512]{1,0:T(8,128)S(1)}, f32[128,512]{1,0:T(8,128)S(1)}, u32[]{:S(2)}, u32[]{:S(2)}) collective-permute-start(f32[128,512]{1,0:T(8,128)S(1)} %convolution_select_fusion.8), channel_id=1, source_target_pairs={{0,32},{4,36},{8,40},{12,44},{16,48},{20,52},{24,56},{28,60},{32,6... | collective-permute-start | bytes 786440 | tf_op jit(solution)/shard_map/ppermute | solution.py:10
  281.2 0.7 copy-start.7
  282.0 68.9 %all-gather.31.cloned.1.call-start = ((), (), s32[]{:S(2)}) async-start(), calls=%async_computation.12 | async-start | bytes 1310720 | tf_op jit(solution)/shard_map/all_gather | solution.py:88
  295.1 15.1 %collective-permute-start.22 = (f32[128,512]{1,0:T(8,128)S(1)}, f32[128,512]{1,0:T(8,128)S(1)}, u32[]{:S(2)}, u32[]{:S(2)}) collective-permute-start(f32[128,512]{1,0:T(8,128)S(1)} %convolution_select_fusion.3), channel_id=1, source_target_pairs={{16,0},{20,4},{24,8},{28,12},{32,16},{36,20},{40,24},{44,28},{48,3... | collective-permute-start | bytes 786440 | tf_op jit(solution)/shard_map/ppermute | solution.py:10
  310.3 0.7 copy-start.8
  311.0 68.8 %all-gather.23.cloned.1.call-start = ((), (), s32[]{:S(2)}) async-start(), calls=%async_computation.8 | async-start | bytes 1310720 | tf_op jit(solution)/shard_map/all_gather | solution.py:88
  324.0 8.3 %collective-permute-start.12 = (f32[128,512]{1,0:T(8,128)S(1)}, f32[128,512]{1,0:T(8,128)S(1)}, u32[]{:S(2)}, u32[]{:S(2)}) collective-permute-start(f32[128,512]{1,0:T(8,128)S(1)} %convolution_select_fusion.7), channel_id=1, source_target_pairs={{0,64},{4,68},{8,72},{12,76},{16,80},{20,84},{24,88},{28,92},{32,9... | collective-permute-start | bytes 786440 | tf_op jit(solution)/shard_map/ppermute | solution.py:10
  332.3 0.7 copy-start.9
  333.0 156.7 %all-gather.33.cloned.1.call-start = ((), (), s32[]{:S(2)}) async-start(), calls=%async_computation.13 | async-start | bytes 1310720 | tf_op jit(solution)/shard_map/all_gather | solution.py:88
  352.9 16.8 %collective-permute-start.24 = (f32[128,512]{1,0:T(8,128)S(1)}, f32[128,512]{1,0:T(8,128)}, u32[]{:S(2)}, u32[]{:S(2)}) collective-permute-start(f32[128,512]{1,0:T(8,128)S(1)} %convolution_select_fusion.2), channel_id=1, source_target_pairs={{32,0},{36,4},{40,8},{44,12},{48,16},{52,20},{56,24},{60,28},{64,3... | collective-permute-start | bytes 786440 | tf_op jit(solution)/shard_map/ppermute | solution.py:10
  369.7 136.1 %all-gather.25.cloned.1.call-start = ((), (), s32[]{:S(2)}) async-start(), calls=%async_computation.9 | async-start | bytes 1310720 | tf_op jit(solution)/shard_map/all_gather | solution.py:88
  381.7 0.7 copy-start.1
  382.4 7.9 %collective-permute-start.13 = (f32[128,512]{1,0:T(8,128)S(1)}, f32[128,512]{1,0:T(8,128)}, u32[]{:S(2)}, u32[]{:S(2)}) collective-permute-start(f32[128,512]{1,0:T(8,128)S(1)} %convolution_select_fusion.6), channel_id=1, source_target_pairs={{0,128},{4,132},{8,136},{12,140},{16,144},{20,148},{24,152},{28,15... | collective-permute-start | bytes 786440 | tf_op jit(solution)/shard_map/ppermute | solution.py:10
  387.1 7.0 collective-permute-start
  394.1 7.0 collective-permute-start.1
  411.8 7.7 collective-permute-start.3
  430.3 8.6 %collective-permute-start.5 = (f32[4,128]{1,0:T(4,128)S(1)}, f32[4,128]{1,0:T(4,128)S(1)}, u32[]{:S(2)}, u32[]{:S(2)}) collective-permute-start(f32[4,128]{1,0:T(4,128)S(1)} %fusion.33), channel_id=1, source_target_pairs={{0,16},{4,20},{8,24},{12,28},{16,32},{20,36},{24,40},{28,44},{32,4... | collective-permute-start | bytes 6152 | tf_op jit(solution)/shard_map/ppermute | solution.py:10
  449.6 10.4 %collective-permute-start.7 = (f32[4,128]{1,0:T(4,128)S(1)}, f32[4,128]{1,0:T(4,128)S(1)}, u32[]{:S(2)}, u32[]{:S(2)}) collective-permute-start(f32[4,128]{1,0:T(4,128)S(1)} %fusion.32), channel_id=1, source_target_pairs={{0,32},{4,36},{8,40},{12,44},{16,48},{20,52},{24,56},{28,60},{32,6... | collective-permute-start | bytes 6152 | tf_op jit(solution)/shard_map/ppermute | solution.py:10
  470.7 5.5 collective-permute-start.9
  487.2 18.6 %copy-start.2 = (f32[128,512]{1,0:T(8,128)S(1)}, f32[128,512]{1,0:T(8,128)}, u32[]{:S(2)}) copy-start(f32[128,512]{1,0:T(8,128)} %copy-done.1) | copy-start | bytes 786436
  487.2 8.1 %collective-permute-start.11 = (f32[4,128]{1,0:T(4,128)S(1)}, f32[4,128]{1,0:T(4,128)S(1)}, u32[]{:S(2)}, u32[]{:S(2)}) collective-permute-start(f32[4,128]{1,0:T(4,128)S(1)} %fusion.30), channel_id=1, source_target_pairs={{0,128},{4,132},{8,136},{12,140},{16,144},{20,148},{24,152},{28,15... | collective-permute-start | bytes 6152 | tf_op jit(solution)/shard_map/ppermute | solution.py:10
  491.7 21.0 %collective-permute-start.26 = (f32[128,512]{1,0:T(8,128)S(1)}, f32[128,512]{1,0:T(8,128)S(1)}, u32[]{:S(2)}, u32[]{:S(2)}) collective-permute-start(f32[128,512]{1,0:T(8,128)S(1)} %convolution_select_fusion.1), channel_id=1, source_target_pairs={{64,0},{68,4},{72,8},{76,12},{80,16},{84,20},{88,24},{92,28},{96,3... | collective-permute-start | bytes 786440 | tf_op jit(solution)/shard_map/ppermute | solution.py:10
  509.0 8.9 %all-to-all-start = ((f32[4,1,128]{2,1,0:T(1,128)}), f32[4,1,128]{2,1,0:T(1,128)S(1)}, u32[]{:S(2)}, u32[]{:S(2)}) async-start(f32[4,1,128]{2,1,0:T(1,128)} %bitcast.18), calls=%async_computation | async-start | bytes 4096 | tf_op jit(solution)/shard_map/all_to_all | solution.py:100
  512.6 192.4 %all-gather.35.cloned.1.call-start = ((), (), s32[]{:S(2)}) async-start(), calls=%async_computation.14 | async-start | bytes 1310720 | tf_op jit(solution)/shard_map/all_gather | solution.py:88
  512.7 0.7 copy-start.5
  573.2 1.0 copy-start.4
  612.8 3.2 collective-permute-start.14
  616.0 7.0 collective-permute-start.15
  633.6 5.5 collective-permute-start.17
  650.0 6.4 collective-permute-start.19
  667.1 9.5 %collective-permute-start.21 = (f32[4,128]{1,0:T(4,128)S(1)}, f32[4,128]{1,0:T(4,128)S(1)}, u32[]{:S(2)}, u32[]{:S(2)}) collective-permute-start(f32[4,128]{1,0:T(4,128)S(1)} %fusion.25), channel_id=1, source_target_pairs={{32,0},{36,4},{40,8},{44,12},{48,16},{52,20},{56,24},{60,28},{64,3... | collective-permute-start | bytes 6152 | tf_op jit(solution)/shard_map/ppermute | solution.py:10
  687.4 5.5 collective-permute-start.23
  703.6 7.1 collective-permute-start.25
  760.5 0.6 copy-start.14
Sparse Core Ops, SparseCore 0:
  9.8 29.4 all-gather.12
  143.0 24.5 all-gather.14
  180.8 26.2 all-gather.16
  208.7 27.0 all-gather.26
  237.4 27.0 all-gather.18
  266.1 27.0 all-gather.28
  295.0 27.0 all-gather.20
  323.9 27.0 all-gather.30
  352.7 27.0 all-gather.22
  381.4 27.0 all-gather.32
  410.3 27.0 all-gather.24
  514.9 23.5 all-gather.34
where the time goes:
time: 770 us; the launch traced here: 768 us
  waiting for transfers between devices  285 us (37%)
  blocking collectives  142 us (18%)
  matrix products  117 us (15%)
  starting transfers between devices  91.9 us (12%)
  local copies, waits for them, and re-layouts  61 us (8%)
  other arithmetic  53.3 us (7%)
  between operations  14.8 us (2%)
    ppermute x27, waiting for transfers between devices, passed_along(): return lax.ppermute(block, axis, route)  127 us
    all_gather x12, blocking collectives, doubling(): lax.all_gather(arrived[1], 'state', axis=1, tiled=True)  126 us
    all_gather x11, waiting for transfers between devices, doubling(): lax.all_gather(arrived[0], 'state', axis=0, tiled=True)  124 us
    ppermute x27, starting transfers between devices, passed_along(): return lax.ppermute(block, axis, route)  87.8 us
    dot_general x46, matrix products, transposed(): lax.dot_general(left, right, (((1,), (1,)), ((), ())), precision=lax.Prec...  59.6 us
    dot_general x76, matrix products, product(): jnp.dot(left, right, precision=lax.Precision.HIGHEST, preferred_element_t...  57.1 us
    dynamic_slice x112, local copies, waits for them, and re-layouts, per_device(): lax.scan(filter_portion, (owned_rows, initial_shifts), (observed_masks, s...  49.2 us
    all_gather x1, waiting for transfers between devices, per_device(): lax.all_gather(dynamics, 'state', axis=0, tiled=True) * block_mask  29 us
  transfers between devices with their start and end apart: 40, of which 34 were waited for; matrix products, arithmetic and copies ran while one was open for 19% of the time, Pallas kernels for 0%

commit v1 on v0

--- a/solution.py
+++ b/solution.py
@@ -2,6 +2,27 @@
 import jax.numpy as jnp
 from jax import lax
 from jax.sharding import PartitionSpec as P
+
+
+def ring_gather(x, axis, dim):
+    length, index, span = (lax.axis_size(axis), lax.axis_index(axis), x.shape[dim])
+    right = [(i, (i + 1) % length) for i in range(length)]
+    downward = [(i, (i - 1) % length) for i in range(length)]
+    filled = jnp.zeros((*x.shape[:dim], length * span, *x.shape[dim + 1 :]), x.dtype)
+    filled = lax.dynamic_update_slice_in_dim(filled, x, index * span, axis=dim)
+    from_left = from_right = x
+    half = length // 2
+    for hop in range(1, half + 1):
+        from_left = lax.ppermute(from_left, axis, right)
+        filled = lax.dynamic_update_slice_in_dim(
+            filled, from_left, (index - hop) % length * span, axis=dim
+        )
+        if hop < length - half:
+            from_right = lax.ppermute(from_right, axis, downward)
+            filled = lax.dynamic_update_slice_in_dim(
+                filled, from_right, (index + hop) % length * span, axis=dim
+            )
+    return filled
 
 
 def passed_along(block, axis, distance):
@@ -85,7 +106,7 @@
                 current = select_tree(usable, arrived, identity)
             else:
                 gathered = (
-                    lax.all_gather(arrived[0], "state", axis=0, tiled=True),
+                    ring_gather(arrived[0], "state", 0),
                     lax.all_gather(arrived[1], "state", axis=1, tiled=True),
                 )
                 current = select_tree(usable, combine_rows(gathered, current), current)

time: 770 us -> 667 us (0.87); the launches traced: 768 us -> 656 us
  waiting for transfers between devices: 285 us -> 151 us
  starting transfers between devices: 91.9 us -> 129 us
  matrix products: 117 us -> 103 us
    all_gather x11 -> x0, waiting for transfers between devices: 124 us -> none  [doubling(): lax.all_gather(arrived[0], 'state', axis=0, tiled=True)]
    ppermute x27, waiting for transfers between devices: 127 us -> 64.6 us  [passed_along(): return lax.ppermute(block, axis, route)]
    ppermute x0 -> x33, waiting for transfers between devices: none -> 55.9 us  [the longest x22 55.9 us: ring_gather(): from_left = lax.ppermute(from_left, axis, right)]
    ppermute x0 -> x33, starting transfers between devices: none -> 39.4 us  [the longest x11 20.3 us: ring_gather(): from_right = lax.ppermute(from_right, axis, downward)]
    dot_general x76, matrix products: 57.1 us -> 43.6 us  [product(): jnp.dot(left, right, precision=lax.Precision.HIGHEST, preferred_element_t...]
  transfers between devices with their start and end apart: 40 -> 62, of which waited for: 34 -> 31; matrix products, arithmetic and copies ran while one was open for 19% -> 21% of each run, Pallas kernels for 0% -> 0%
where the time goes in v1:
time: 667 us; the launch traced here: 656 us
  waiting for transfers between devices  151 us (23%)
  blocking collectives  145 us (22%)
  starting transfers between devices  129 us (19%)
  matrix products  103 us (15%)
  local copies, waits for them, and re-layouts  57.3 us (9%)
  other arithmetic  53.3 us (8%)
  between operations  15.4 us (2%)
    all_gather x12, blocking collectives, doubling(): lax.all_gather(arrived[1], 'state', axis=1, tiled=True)  126 us
    ppermute x27, starting transfers between devices, passed_along(): return lax.ppermute(block, axis, route)  86.1 us
    ppermute x27, waiting for transfers between devices, passed_along(): return lax.ppermute(block, axis, route)  64.6 us
    dot_general x46, matrix products, transposed(): lax.dot_general(left, right, (((1,), (1,)), ((), ())), precision=lax.Prec...  59.6 us
    ppermute x22, waiting for transfers between devices, ring_gather(): from_left = lax.ppermute(from_left, axis, right)  55.9 us
    dynamic_slice x112, local copies, waits for them, and re-layouts, per_device(): lax.scan(filter_portion, (owned_rows, initial_shifts), (observed_masks, s...  48.4 us
    dot_general x76, matrix products, product(): jnp.dot(left, right, precision=lax.Precision.HIGHEST, preferred_element_t...  43.6 us
    all_gather x1, waiting for transfers between devices, per_device(): lax.all_gather(dynamics, 'state', axis=0, tiled=True) * block_mask  29 us
  transfers between devices with their start and end apart: 62, of which 31 were waited for; matrix products, arithmetic and copies ran while one was open for 21% of the time, Pallas kernels for 0%

profile of v1, /device:TPU:8, one launch (start us, length us, event | category | flops | bytes accessed | tf_op | source)
XLA Modules:
  0.0 656.1 jit_solution(11681607745434436850)
XLA Ops:
  10.3 29.0 %all-gather.2.cloned.1.call-done = f32[512,512]{1,0:T(8,128)} async-done(((f32[128,512]{1,0:T(8,128)}), f32[512,512]{1,0:T(8,128)}) %all-gather.2.cloned.1.call-update) | async-done | bytes 1048592 | tf_op jit(solution)/shard_map/all_gather | solution.py:70
  40.8 39.6 %while.71 = (s32[]{:T(128)}, f32[128,512]{1,0:T(8,128)S(1)}, f32[16]{0:T(128)S(1)}, f32[16,512]{1,0:T(8,128)S(1)}, f32[512,512]{1,0:T(8,128)S(1)}, /*index=5*/s32[]{:T(128)}) while((s32[]{:T(128)}, f32[128,512]{1,0:T(8,128)S(1)}, f32[16]{0:T(128)S(1)}, f32[16,512]{1,0:T(8,128)S(1)}, f32[512,512]{1,0:T(8,128)S(1)}, /*index=5*/s32[]{:T(128)}) %tuple.143), condition=%wide.region_7.8_spmd, body=%wide.region_6.7_spmd.sunk | while | flops 402784256 | bytes 2103393 | solution.py:176
  80.4 2.6 collective-permute-start.34
  83.0 38.8 %while.73 = (s32[]{:T(128)}, f32[128,512]{1,0:T(8,128)S(1)}, f32[4,128]{1,0:T(4,128)S(1)}, f32[16,512]{1,0:T(8,128)S(1)}, f32[512,512]{1,0:T(8,128)S(1)}, /*inde...) while((s32[]{:T(128)}, f32[128,512]{1,0:T(8,128)S(1)}, ...), condition=%wide.region_1.2_spmd.clone, body=%wide.region_0.1_spmd.clone.sunk | while | flops 403506688 | bytes 2372823 | solution.py:132
  123.7 7.9 %collective-permute-done.2 = f32[128,512]{1,0:T(8,128)S(1)} collective-permute-done((f32[128,512]{1,0:T(8,128)S(1)}, f32[128,512]{1,0:T(8,128)S(1)}, u32[]{:S(2)}, u32[]{:S(2)}) %collective-permute-start.2) | collective-permute-done | bytes 262176 | tf_op jit(solution)/shard_map/ppermute | solution.py:31
  133.6 5.8 collective-permute-start.36
  144.0 2.4 collective-permute-start.6
  147.5 4.3 collective-permute-done.5
  151.8 5.6 collective-permute-done.37
  157.6 3.5 collective-permute-done.7
  165.8 4.8 collective-permute-start.41
  172.6 5.0 collective-permute-done
  179.6 5.1 collective-permute-done.1
  184.6 10.4 %all_gather.40 = f32[4,512]{1,0:T(4,128)S(1)} all-gather(f32[4,128]{1,0:T(4,128)S(1)} %collective-permute-done.1), channel_id=1, replica_groups=mesh['tm'=64,'state'=4] {'state'}, dimensions={1}, use_global_device_ids=true | all-gather | bytes 10240 | tf_op jit(solution)/shard_map/all_gather | solution.py:110
  195.2 2.4 collective-permute-start.42
  200.0 5.2 collective-permute-done.42
  205.4 2.7 collective-permute-done.12
  213.6 4.9 collective-permute-start.46
  218.4 3.7 collective-permute-done.14
  225.1 5.7 collective-permute-done.3
  230.8 10.9 %all_gather.41 = f32[4,512]{1,0:T(4,128)S(1)} all-gather(f32[4,128]{1,0:T(4,128)S(1)} %collective-permute-done.3), channel_id=1, replica_groups=mesh['tm'=64,'state'=4] {'state'}, dimensions={1}, use_global_device_ids=true | all-gather | bytes 10240 | tf_op jit(solution)/shard_map/all_gather | solution.py:110
  245.7 6.6 collective-permute-done.8
  252.3 10.4 %all_gather.42 = f32[4,512]{1,0:T(4,128)S(1)} all-gather(f32[4,128]{1,0:T(4,128)S(1)} %collective-permute-done.8), channel_id=1, replica_groups=mesh['tm'=64,'state'=4] {'state'}, dimensions={1}, use_global_device_ids=true | all-gather | bytes 10240 | tf_op jit(solution)/shard_map/all_gather | solution.py:110
  262.8 3.2 collective-permute-start.48
  267.2 6.6 %collective-permute-done.17 = f32[128,512]{1,0:T(8,128)S(1)} collective-permute-done((f32[128,512]{1,0:T(8,128)}, f32[128,512]{1,0:T(8,128)S(1)}, u32[]{:S(2)}, u32[]{:S(2)}) %collective-permute-start.17) | collective-permute-done | bytes 262176 | tf_op jit(solution)/shard_map/ppermute | solution.py:16
  276.9 8.6 %collective-permute-start.13 = (f32[4,128]{1,0:T(4,128)S(1)}, f32[4,128]{1,0:T(4,128)S(1)}, u32[]{:S(2)}, u32[]{:S(2)}) collective-permute-start(f32[4,128]{1,0:T(4,128)S(1)} %fusion.32), channel_id=1, source_target_pairs={{0,32},{4,36},{8,40},{12,44},{16,48},{20,52},{24,56},{28,60},{32,6... | collective-permute-start | bytes 6152 | tf_op jit(solution)/shard_map/ppermute | solution.py:31
  285.6 4.5 collective-permute-done.13
  290.0 10.4 %all_gather.43 = f32[4,512]{1,0:T(4,128)S(1)} all-gather(f32[4,128]{1,0:T(4,128)S(1)} %collective-permute-done.13), channel_id=1, replica_groups=mesh['tm'=64,'state'=4] {'state'}, dimensions={1}, use_global_device_ids=true | all-gather | bytes 10240 | tf_op jit(solution)/shard_map/all_gather | solution.py:110
  300.7 2.4 collective-permute-start.20
  304.3 3.7 collective-permute-done.49
  308.1 2.8 collective-permute-done.20
  311.6 6.8 %collective-permute-done.22 = f32[128,512]{1,0:T(8,128)S(1)} collective-permute-done((f32[128,512]{1,0:T(8,128)S(1)}, f32[128,512]{1,0:T(8,128)S(1)}, u32[]{:S(2)}, u32[]{:S(2)}) %collective-permute-start.22) | collective-permute-done | bytes 262176 | tf_op jit(solution)/shard_map/ppermute | solution.py:16
  319.2 3.3 collective-permute-start.24
  323.3 5.0 collective-permute-start.51
  328.6 3.1 collective-permute-start.18
  331.8 3.3 collective-permute-start.26
  335.1 10.6 %all_gather.44 = f32[4,512]{1,0:T(4,128)S(1)} all-gather(f32[4,128]{1,0:T(4,128)S(1)} %collective-permute-done.18), channel_id=1, replica_groups=mesh['tm'=64,'state'=4] {'state'}, dimensions={1}, use_global_device_ids=true | all-gather | bytes 10240 | tf_op jit(solution)/shard_map/all_gather | solution.py:110
  350.2 6.2 collective-permute-done.27
  364.0 6.0 collective-permute-start.23
  370.0 2.7 collective-permute-start.30
  372.7 10.5 %all_gather.45 = f32[4,512]{1,0:T(4,128)S(1)} all-gather(f32[4,128]{1,0:T(4,128)S(1)} %collective-permute-done.23), channel_id=1, replica_groups=mesh['tm'=64,'state'=4] {'state'}, dimensions={1}, use_global_device_ids=true | all-gather | bytes 10240 | tf_op jit(solution)/shard_map/all_gather | solution.py:110
  383.3 2.6 collective-permute-start.31
  386.1 5.0 collective-permute-done.31
  393.0 3.2 all-to-all-start
  397.0 4.1 collective-permute-start.56
  401.5 55.4 %while.70 = (s32[]{:T(128)}, f32[1,512]{1,0:T(1,128)S(1)}, f32[16,1,512]{2,1,0:T(1,128)S(1)}, f32[512,512]{1,0:T(8,128)S(1)}, f32[16,512]{1,0:T(8,128)S(1)}, /*i...) while((s32[]{:T(128)}, f32[1,512]{1,0:T(1,128)S(1)}, ...), condition=%wide.region_3.4_spmd, body=%wide.region_2.3_spmd.sunk | while | flops 3147267 | bytes 1063049 | solution.py:148
  458.5 30.2 %while.74 = (s32[]{:T(128)}, f32[1,512]{1,0:T(1,128)S(1)}, f32[16]{0:T(128)S(1)}, f32[512,512]{1,0:T(8,128)S(1)}, f32[16,512]{1,0:T(8,128)S(1)}, /*index=5*/f32[...) while((s32[]{:T(128)}, f32[1,512]{1,0:T(1,128)S(1)}, f32[16]{0:T(128)S(1)}, ...), condition=%wide.region_5.6_spmd.clone, body=%wide.region_4.5_spmd.clone.sunk | while | flops 3147780 | bytes 1065103 | solution.py:167
  488.8 9.6 %all_to_all.48 = f32[1,4,128]{2,0,1:T(1,128)S(1)} all-to-all(f32[1,4,128]{2,0,1:T(1,128)S(1)} %bitcast.186), channel_id=1, replica_groups=mesh['tm'=64,'state'=4] {'state'}, dimensions={1} | all-to-all | bytes 4096 | tf_op jit(solution)/shard_map/all_to_all | solution.py:170
  501.5 5.7 collective-permute-start.33
  507.9 2.7 collective-permute-start.58
  510.6 10.6 %all_gather.46 = f32[4,512]{1,0:T(4,128)S(1)} all-gather(f32[4,128]{1,0:T(4,128)S(1)} %collective-permute-done.33), channel_id=1, replica_groups=mesh['tm'=64,'state'=4] {'state'}, dimensions={1}, use_global_device_ids=true | all-gather | bytes 10240 | tf_op jit(solution)/shard_map/all_gather | solution.py:110
  523.5 2.4 collective-permute-start.59
  526.9 10.6 %all_gather.47 = f32[4,512]{1,0:T(4,128)S(1)} all-gather(f32[4,128]{1,0:T(4,128)S(1)} %collective-permute-done.35), channel_id=1, replica_groups=mesh['tm'=64,'state'=4] {'state'}, dimensions={1}, use_global_device_ids=true | all-gather | bytes 10240 | tf_op jit(solution)/shard_map/all_gather | solution.py:110
  539.8 4.4 collective-permute-done.40
  544.3 10.6 %all_gather.48 = f32[4,512]{1,0:T(4,128)S(1)} all-gather(f32[4,128]{1,0:T(4,128)S(1)} %collective-permute-done.40), channel_id=1, replica_groups=mesh['tm'=64,'state'=4] {'state'}, dimensions={1}, use_global_device_ids=true | all-gather | bytes 10240 | tf_op jit(solution)/shard_map/all_gather | solution.py:110
  555.1 3.3 collective-permute-start.45
  558.4 6.1 collective-permute-done.45
  564.5 10.4 %all_gather.49 = f32[4,512]{1,0:T(4,128)S(1)} all-gather(f32[4,128]{1,0:T(4,128)S(1)} %collective-permute-done.45), channel_id=1, replica_groups=mesh['tm'=64,'state'=4] {'state'}, dimensions={1}, use_global_device_ids=true | all-gather | bytes 10240 | tf_op jit(solution)/shard_map/all_gather | solution.py:110
  577.2 3.5 collective-permute-done.50
  580.7 10.6 %all_gather.50 = f32[4,512]{1,0:T(4,128)S(1)} all-gather(f32[4,128]{1,0:T(4,128)S(1)} %collective-permute-done.50), channel_id=1, replica_groups=mesh['tm'=64,'state'=4] {'state'}, dimensions={1}, use_global_device_ids=true | all-gather | bytes 10240 | tf_op jit(solution)/shard_map/all_gather | solution.py:110
  593.6 5.0 collective-permute-done.55
  598.6 10.4 %all_gather.51 = f32[4,512]{1,0:T(4,128)S(1)} all-gather(f32[4,128]{1,0:T(4,128)S(1)} %collective-permute-done.55), channel_id=1, replica_groups=mesh['tm'=64,'state'=4] {'state'}, dimensions={1}, use_global_device_ids=true | all-gather | bytes 10240 | tf_op jit(solution)/shard_map/all_gather | solution.py:110
  609.3 8.9 %all_to_all.49 = f32[4,1,128]{2,1,0:T(1,128)S(1)} all-to-all(f32[4,1,128]{2,1,0:T(1,128)S(1)} %bitcast.189), channel_id=1, replica_groups=mesh['tm'=64,'state'=4] {'state'}, dimensions={0} | all-to-all | bytes 4096 | tf_op jit(solution)/shard_map/all_to_all | solution.py:121
  618.1 30.3 %while.72 = (s32[]{:T(128)}, f32[1,512]{1,0:T(1,128)S(1)}, f32[16,1,512]{2,1,0:T(1,128)S(1)}, f32[16]{0:T(128)S(1)}, f32[512,512]{1,0:T(8,128)S(1)}, /*index=5*/...) while((s32[]{:T(128)}, f32[1,512]{1,0:T(1,128)S(1)}, f32[16,1,512]{2,1,0:T(1,128)S(1)}, ...), condition=%wide.region_9.10_spmd, body=%wide.region_8.9_spmd.sunk | while | flops 3147267 | bytes 1067141 | solution.py:180
  (566 shorter events, 270.0 us)
Async XLA Ops:
  7.2 384.6 %copy-start = (f32[4,512]{1,0:T(4,128)S(1)}, f32[4,512]{1,0:T(4,128)}, u32[]{:S(2)}) copy-start(f32[4,512]{1,0:T(4,128)} %param.18) | copy-start | bytes 24580
  7.2 32.2 %all-gather.2.cloned.1.call-start = ((), (), s32[]{:S(2)}) async-start(), calls=%async_computation.3 | async-start | bytes 1310720 | tf_op jit(solution)/shard_map/all_gather | solution.py:70
  39.3 1.2 copy-start.1
  80.4 43.3 %collective-permute-start.34 = (f32[128,512]{1,0:T(8,128)S(1)}, f32[128,512]{1,0:T(8,128)S(1)}, u32[]{:S(2)}, u32[]{:S(2)}) collective-permute-start(f32[128,512]{1,0:T(8,128)S(1)} %get-tuple-element.499), channel_id=1, source_target_pairs={{4,0},{8,4},{12,8},{16,12},{20,16},{24,20},{28,24},{32,28},{36,32}... | collective-permute-start | bytes 786440 | tf_op jit(solution)/shard_map/ppermute | solution.py:31
  121.7 9.8 %collective-permute-start.2 = (f32[128,512]{1,0:T(8,128)S(1)}, f32[128,512]{1,0:T(8,128)S(1)}, u32[]{:S(2)}, u32[]{:S(2)}) collective-permute-start(f32[128,512]{1,0:T(8,128)S(1)} %get-tuple-element.496), channel_id=1, source_target_pairs={{0,4},{4,8},{8,12},{12,16},{16,20},{20,24},{24,28},{28,32},{32,36}... | collective-permute-start | bytes 786440 | tf_op jit(solution)/shard_map/ppermute | solution.py:31
  131.6 9.8 %collective-permute-start.4 = (f32[128,512]{1,0:T(8,128)S(1)}, f32[128,512]{1,0:T(8,128)S(1)}, u32[]{:S(2)}, u32[]{:S(2)}) collective-permute-start(f32[128,512]{1,0:T(8,128)S(1)} %get-tuple-element.664), channel_id=1, source_target_pairs={{0,4},{4,8},{8,12},{12,16},{16,20},{20,24},{24,28},{28,32},{32,36}... | collective-permute-start | bytes 786440 | tf_op jit(solution)/shard_map/ppermute | solution.py:31
  133.6 9.6 %collective-permute-start.36 = (f32[128,512]{1,0:T(8,128)S(1)}, f32[128,512]{1,0:T(8,128)S(1)}, u32[]{:S(2)}, u32[]{:S(2)}) collective-permute-start(f32[128,512]{1,0:T(8,128)S(1)} %get-tuple-element.663), channel_id=1, source_target_pairs={{4,0},{8,4},{12,8},{16,12},{20,16},{24,20},{28,24},{32,28},{36,32}... | collective-permute-start | bytes 786440 | tf_op jit(solution)/shard_map/ppermute | solution.py:31
  141.4 10.4 %collective-permute-start.5 = (f32[128,512]{1,0:T(8,128)S(1)}, f32[128,512]{1,0:T(8,128)S(1)}, u32[]{:S(2)}, u32[]{:S(2)}) collective-permute-start(f32[128,512]{1,0:T(8,128)S(1)} %collective-permute-done.4), channel_id=1, source_target_pairs={{0,1},{1,2},{2,3},{3,0},{4,5},{5,6},{6,7},{7,4},{8,9},{9,10},{10,1... | collective-permute-start | bytes 786440 | tf_op jit(solution)/shard_map/ppermute | solution.py:16
  143.2 14.3 %collective-permute-start.37 = (f32[128,512]{1,0:T(8,128)S(1)}, f32[128,512]{1,0:T(8,128)S(1)}, u32[]{:S(2)}, u32[]{:S(2)}) collective-permute-start(f32[128,512]{1,0:T(8,128)S(1)} %collective-permute-done.36), channel_id=1, source_target_pairs={{0,1},{1,2},{2,3},{3,0},{4,5},{5,6},{6,7},{7,4},{8,9},{9,10},{10,1... | collective-permute-start | bytes 786440 | tf_op jit(solution)/shard_map/ppermute | solution.py:16
  144.0 13.5 %collective-permute-start.6 = (f32[128,512]{1,0:T(8,128)S(1)}, f32[128,512]{1,0:T(8,128)S(1)}, u32[]{:S(2)}, u32[]{:S(2)}) collective-permute-start(f32[128,512]{1,0:T(8,128)S(1)} %collective-permute-done.4), channel_id=1, source_target_pairs={{0,3},{1,0},{2,1},{3,2},{4,7},{5,4},{6,5},{7,6},{8,11},{9,8},{10,9... | collective-permute-start | bytes 786440 | tf_op jit(solution)/shard_map/ppermute | solution.py:21
  146.4 11.1 %collective-permute-start.38 = (f32[128,512]{1,0:T(8,128)S(1)}, f32[128,512]{1,0:T(8,128)S(1)}, u32[]{:S(2)}, u32[]{:S(2)}) collective-permute-start(f32[128,512]{1,0:T(8,128)S(1)} %collective-permute-done.36), channel_id=1, source_target_pairs={{0,3},{1,0},{2,1},{3,2},{4,7},{5,4},{6,5},{7,6},{8,11},{9,8},{10,9... | collective-permute-start | bytes 786440 | tf_op jit(solution)/shard_map/ppermute | solution.py:21
  151.8 9.3 %collective-permute-start.7 = (f32[128,512]{1,0:T(8,128)S(1)}, f32[128,512]{1,0:T(8,128)S(1)}, u32[]{:S(2)}, u32[]{:S(2)}) collective-permute-start(f32[128,512]{1,0:T(8,128)S(1)} %collective-permute-done.5), channel_id=1, source_target_pairs={{0,1},{1,2},{2,3},{3,0},{4,5},{5,6},{6,7},{7,4},{8,9},{9,10},{10,1... | collective-permute-start | bytes 786440 | tf_op jit(solution)/shard_map/ppermute | solution.py:16
  157.5 7.6 %collective-permute-start.39 = (f32[128,512]{1,0:T(8,128)S(1)}, f32[128,512]{1,0:T(8,128)S(1)}, u32[]{:S(2)}, u32[]{:S(2)}) collective-permute-start(f32[128,512]{1,0:T(8,128)S(1)} %collective-permute-done.37), channel_id=1, source_target_pairs={{0,1},{1,2},{2,3},{3,0},{4,5},{5,6},{6,7},{7,4},{8,9},{9,10},{10,1... | collective-permute-start | bytes 786440 | tf_op jit(solution)/shard_map/ppermute | solution.py:16
  161.9 10.7 %collective-permute-start.9 = (f32[128,512]{1,0:T(8,128)S(1)}, f32[128,512]{1,0:T(8,128)S(1)}, u32[]{:S(2)}, u32[]{:S(2)}) collective-permute-start(f32[128,512]{1,0:T(8,128)S(1)} %convolution_select_fusion.10), channel_id=1, source_target_pairs={{0,8},{4,12},{8,16},{12,20},{16,24},{20,28},{24,32},{28,36},{32,40... | collective-permute-start | bytes 786440 | tf_op jit(solution)/shard_map/ppermute | solution.py:31
  165.8 29.4 %collective-permute-start.41 = (f32[128,512]{1,0:T(8,128)S(1)}, f32[128,512]{1,0:T(8,128)S(1)}, u32[]{:S(2)}, u32[]{:S(2)}) collective-permute-start(f32[128,512]{1,0:T(8,128)S(1)} %convolution_select_fusion.4), channel_id=1, source_target_pairs={{8,0},{12,4},{16,8},{20,12},{24,16},{28,20},{32,24},{36,28},{40,32... | collective-permute-start | bytes 786440 | tf_op jit(solution)/shard_map/ppermute | solution.py:31
  170.6 7.0 %collective-permute-start = (f32[4,128]{1,0:T(4,128)S(1)}, f32[4,128]{1,0:T(4,128)S(1)}, u32[]{:S(2)}, u32[]{:S(2)}) collective-permute-start(f32[4,128]{1,0:T(4,128)S(1)} %get-tuple-element.495), channel_id=1, source_target_pairs={{0,4},{4,8},{8,12},{12,16},{16,20},{20,24},{24,28},{28,32},{32,36}... | collective-permute-start | bytes 6152 | tf_op jit(solution)/shard_map/ppermute | solution.py:31
  172.5 26.6 %collective-permute-start.10 = (f32[128,512]{1,0:T(8,128)S(1)}, f32[128,512]{1,0:T(8,128)S(1)}, u32[]{:S(2)}, u32[]{:S(2)}) collective-permute-start(f32[128,512]{1,0:T(8,128)S(1)} %collective-permute-done.9), channel_id=1, source_target_pairs={{0,1},{1,2},{2,3},{3,0},{4,5},{5,6},{6,7},{7,4},{8,9},{9,10},{10,1... | collective-permute-start | bytes 786440 | tf_op jit(solution)/shard_map/ppermute | solution.py:16
  177.6 7.0 %collective-permute-start.1 = (f32[4,128]{1,0:T(4,128)S(1)}, f32[4,128]{1,0:T(4,128)S(1)}, u32[]{:S(2)}, u32[]{:S(2)}) collective-permute-start(f32[4,128]{1,0:T(4,128)S(1)} %broadcast_select_fusion.1), channel_id=1, source_target_pairs={{0,4},{4,8},{8,12},{12,16},{16,20},{20,24},{24,28},{28,32},{32,36}... | collective-permute-start | bytes 6152 | tf_op jit(solution)/shard_map/ppermute | solution.py:31
  195.1 10.2 %collective-permute-start.11 = (f32[128,512]{1,0:T(8,128)S(1)}, f32[128,512]{1,0:T(8,128)S(1)}, u32[]{:S(2)}, u32[]{:S(2)}) collective-permute-start(f32[128,512]{1,0:T(8,128)S(1)} %collective-permute-done.9), channel_id=1, source_target_pairs={{0,3},{1,0},{2,1},{3,2},{4,7},{5,4},{6,5},{7,6},{8,11},{9,8},{10,9... | collective-permute-start | bytes 786440 | tf_op jit(solution)/shard_map/ppermute | solution.py:21
  195.2 10.1 %collective-permute-start.42 = (f32[128,512]{1,0:T(8,128)S(1)}, f32[128,512]{1,0:T(8,128)S(1)}, u32[]{:S(2)}, u32[]{:S(2)}) collective-permute-start(f32[128,512]{1,0:T(8,128)S(1)} %collective-permute-done.41), channel_id=1, source_target_pairs={{0,1},{1,2},{2,3},{3,0},{4,5},{5,6},{6,7},{7,4},{8,9},{9,10},{10,1... | collective-permute-start | bytes 786440 | tf_op jit(solution)/shard_map/ppermute | solution.py:16
  197.5 7.8 %collective-permute-start.43 = (f32[128,512]{1,0:T(8,128)S(1)}, f32[128,512]{1,0:T(8,128)S(1)}, u32[]{:S(2)}, u32[]{:S(2)}) collective-permute-start(f32[128,512]{1,0:T(8,128)S(1)} %collective-permute-done.41), channel_id=1, source_target_pairs={{0,3},{1,0},{2,1},{3,2},{4,7},{5,4},{6,5},{7,6},{8,11},{9,8},{10,9... | collective-permute-start | bytes 786440 | tf_op jit(solution)/shard_map/ppermute | solution.py:21
  199.2 8.9 %collective-permute-start.12 = (f32[128,512]{1,0:T(8,128)S(1)}, f32[128,512]{1,0:T(8,128)S(1)}, u32[]{:S(2)}, u32[]{:S(2)}) collective-permute-start(f32[128,512]{1,0:T(8,128)S(1)} %collective-permute-done.10), channel_id=1, source_target_pairs={{0,1},{1,2},{2,3},{3,0},{4,5},{5,6},{6,7},{7,4},{8,9},{9,10},{10,1... | collective-permute-start | bytes 786440 | tf_op jit(solution)/shard_map/ppermute | solution.py:16
  205.2 7.6 %collective-permute-start.44 = (f32[128,512]{1,0:T(8,128)S(1)}, f32[128,512]{1,0:T(8,128)S(1)}, u32[]{:S(2)}, u32[]{:S(2)}) collective-permute-start(f32[128,512]{1,0:T(8,128)S(1)} %collective-permute-done.42), channel_id=1, source_target_pairs={{0,1},{1,2},{2,3},{3,0},{4,5},{5,6},{6,7},{7,4},{8,9},{9,10},{10,1... | collective-permute-start | bytes 786440 | tf_op jit(solution)/shard_map/ppermute | solution.py:16
  208.8 13.4 %collective-permute-start.14 = (f32[128,512]{1,0:T(8,128)S(1)}, f32[128,512]{1,0:T(8,128)S(1)}, u32[]{:S(2)}, u32[]{:S(2)}) collective-permute-start(f32[128,512]{1,0:T(8,128)S(1)} %convolution_select_fusion.9), channel_id=1, source_target_pairs={{0,16},{4,20},{8,24},{12,28},{16,32},{20,36},{24,40},{28,44},{32,4... | collective-permute-start | bytes 786440 | tf_op jit(solution)/shard_map/ppermute | solution.py:31
  213.6 49.2 %collective-permute-start.46 = (f32[128,512]{1,0:T(8,128)S(1)}, f32[128,512]{1,0:T(8,128)S(1)}, u32[]{:S(2)}, u32[]{:S(2)}) collective-permute-start(f32[128,512]{1,0:T(8,128)S(1)} %convolution_select_fusion.3), channel_id=1, source_target_pairs={{16,0},{20,4},{24,8},{28,12},{32,16},{36,20},{40,24},{44,28},{48,3... | collective-permute-start | bytes 786440 | tf_op jit(solution)/shard_map/ppermute | solution.py:31
  222.2 43.8 %collective-permute-start.15 = (f32[128,512]{1,0:T(8,128)S(1)}, f32[128,512]{1,0:T(8,128)}, u32[]{:S(2)}, u32[]{:S(2)}) collective-permute-start(f32[128,512]{1,0:T(8,128)S(1)} %collective-permute-done.14), channel_id=1, source_target_pairs={{0,1},{1,2},{2,3},{3,0},{4,5},{5,6},{6,7},{7,4},{8,9},{9,10},{10,1... | collective-permute-start | bytes 786440 | tf_op jit(solution)/shard_map/ppermute | solution.py:16
  223.1 7.7 %collective-permute-start.3 = (f32[4,128]{1,0:T(4,128)S(1)}, f32[4,128]{1,0:T(4,128)S(1)}, u32[]{:S(2)}, u32[]{:S(2)}) collective-permute-start(f32[4,128]{1,0:T(4,128)S(1)} %fusion.34), channel_id=1, source_target_pairs={{0,8},{4,12},{8,16},{12,20},{16,24},{20,28},{24,32},{28,36},{32,40... | collective-permute-start | bytes 6152 | tf_op jit(solution)/shard_map/ppermute | solution.py:31
  241.7 25.4 %collective-permute-start.16 = (f32[128,512]{1,0:T(8,128)S(1)}, f32[128,512]{1,0:T(8,128)S(1)}, u32[]{:S(2)}, u32[]{:S(2)}) collective-permute-start(f32[128,512]{1,0:T(8,128)S(1)} %collective-permute-done.14), channel_id=1, source_target_pairs={{0,3},{1,0},{2,1},{3,2},{4,7},{5,4},{6,5},{7,6},{8,11},{9,8},{10,9... | collective-permute-start | bytes 786440 | tf_op jit(solution)/shard_map/ppermute | solution.py:21
  243.7 8.6 %collective-permute-start.8 = (f32[4,128]{1,0:T(4,128)S(1)}, f32[4,128]{1,0:T(4,128)S(1)}, u32[]{:S(2)}, u32[]{:S(2)}) collective-permute-start(f32[4,128]{1,0:T(4,128)S(1)} %fusion.33), channel_id=1, source_target_pairs={{0,16},{4,20},{8,24},{12,28},{16,32},{20,36},{24,40},{28,44},{32,4... | collective-permute-start | bytes 6152 | tf_op jit(solution)/shard_map/ppermute | solution.py:31
  262.7 37.7 %collective-permute-start.47 = (f32[128,512]{1,0:T(8,128)S(1)}, f32[128,512]{1,0:T(8,128)S(1)}, u32[]{:S(2)}, u32[]{:S(2)}) collective-permute-start(f32[128,512]{1,0:T(8,128)S(1)} %collective-permute-done.46), channel_id=1, source_target_pairs={{0,1},{1,2},{2,3},{3,0},{4,5},{5,6},{6,7},{7,4},{8,9},{9,10},{10,1... | collective-permute-start | bytes 786440 | tf_op jit(solution)/shard_map/ppermute | solution.py:16
  262.8 40.3 %collective-permute-start.48 = (f32[128,512]{1,0:T(8,128)S(1)}, f32[128,512]{1,0:T(8,128)S(1)}, u32[]{:S(2)}, u32[]{:S(2)}) collective-permute-start(f32[128,512]{1,0:T(8,128)S(1)} %collective-permute-done.46), channel_id=1, source_target_pairs={{0,3},{1,0},{2,1},{3,2},{4,7},{5,4},{6,5},{7,6},{8,11},{9,8},{10,9... | collective-permute-start | bytes 786440 | tf_op jit(solution)/shard_map/ppermute | solution.py:21
  266.0 7.8 %collective-permute-start.17 = (f32[128,512]{1,0:T(8,128)}, f32[128,512]{1,0:T(8,128)S(1)}, u32[]{:S(2)}, u32[]{:S(2)}) collective-permute-start(f32[128,512]{1,0:T(8,128)} %collective-permute-done.15), channel_id=1, source_target_pairs={{0,1},{1,2},{2,3},{3,0},{4,5},{5,6},{6,7},{7,4},{8,9},{9,10},{10,1... | collective-permute-start | bytes 786440 | tf_op jit(solution)/shard_map/ppermute | solution.py:16
  274.5 26.1 %collective-permute-start.19 = (f32[128,512]{1,0:T(8,128)S(1)}, f32[128,512]{1,0:T(8,128)S(1)}, u32[]{:S(2)}, u32[]{:S(2)}) collective-permute-start(f32[128,512]{1,0:T(8,128)S(1)} %convolution_select_fusion.8), channel_id=1, source_target_pairs={{0,32},{4,36},{8,40},{12,44},{16,48},{20,52},{24,56},{28,60},{32,6... | collective-permute-start | bytes 786440 | tf_op jit(solution)/shard_map/ppermute | solution.py:31
  276.9 13.1 %collective-permute-start.13 = (f32[4,128]{1,0:T(4,128)S(1)}, f32[4,128]{1,0:T(4,128)S(1)}, u32[]{:S(2)}, u32[]{:S(2)}) collective-permute-start(f32[4,128]{1,0:T(4,128)S(1)} %fusion.32), channel_id=1, source_target_pairs={{0,32},{4,36},{8,40},{12,44},{16,48},{20,52},{24,56},{28,60},{32,6... | collective-permute-start | bytes 6152 | tf_op jit(solution)/shard_map/ppermute | solution.py:31
  300.4 7.6 %collective-permute-start.49 = (f32[128,512]{1,0:T(8,128)S(1)}, f32[128,512]{1,0:T(8,128)S(1)}, u32[]{:S(2)}, u32[]{:S(2)}) collective-permute-start(f32[128,512]{1,0:T(8,128)S(1)} %collective-permute-done.47), channel_id=1, source_target_pairs={{0,1},{1,2},{2,3},{3,0},{4,5},{5,6},{6,7},{7,4},{8,9},{9,10},{10,1... | collective-permute-start | bytes 786440 | tf_op jit(solution)/shard_map/ppermute | solution.py:16
  300.7 10.2 %collective-permute-start.20 = (f32[128,512]{1,0:T(8,128)S(1)}, f32[128,512]{1,0:T(8,128)S(1)}, u32[]{:S(2)}, u32[]{:S(2)}) collective-permute-start(f32[128,512]{1,0:T(8,128)S(1)} %collective-permute-done.19), channel_id=1, source_target_pairs={{0,1},{1,2},{2,3},{3,0},{4,5},{5,6},{6,7},{7,4},{8,9},{9,10},{10,1... | collective-permute-start | bytes 786440 | tf_op jit(solution)/shard_map/ppermute | solution.py:16
  303.2 8.4 %collective-permute-start.21 = (f32[128,512]{1,0:T(8,128)S(1)}, f32[128,512]{1,0:T(8,128)S(1)}, u32[]{:S(2)}, u32[]{:S(2)}) collective-permute-start(f32[128,512]{1,0:T(8,128)S(1)} %collective-permute-done.19), channel_id=1, source_target_pairs={{0,3},{1,0},{2,1},{3,2},{4,7},{5,4},{6,5},{7,6},{8,11},{9,8},{10,9... | collective-permute-start | bytes 786440 | tf_op jit(solution)/shard_map/ppermute | solution.py:21
  310.9 7.6 %collective-permute-start.22 = (f32[128,512]{1,0:T(8,128)S(1)}, f32[128,512]{1,0:T(8,128)S(1)}, u32[]{:S(2)}, u32[]{:S(2)}) collective-permute-start(f32[128,512]{1,0:T(8,128)S(1)} %collective-permute-done.20), channel_id=1, source_target_pairs={{0,1},{1,2},{2,3},{3,0},{4,5},{5,6},{6,7},{7,4},{8,9},{9,10},{10,1... | collective-permute-start | bytes 786440 | tf_op jit(solution)/shard_map/ppermute | solution.py:16
  319.2 9.1 %collective-permute-start.24 = (f32[128,512]{1,0:T(8,128)S(1)}, f32[128,512]{1,0:T(8,128)S(1)}, u32[]{:S(2)}, u32[]{:S(2)}) collective-permute-start(f32[128,512]{1,0:T(8,128)S(1)} %convolution_select_fusion.7), channel_id=1, source_target_pairs={{0,64},{4,68},{8,72},{12,76},{16,80},{20,84},{24,88},{28,92},{32,9... | collective-permute-start | bytes 786440 | tf_op jit(solution)/shard_map/ppermute | solution.py:31
  323.3 22.4 %collective-permute-start.51 = (f32[128,512]{1,0:T(8,128)S(1)}, f32[128,512]{1,0:T(8,128)}, u32[]{:S(2)}, u32[]{:S(2)}) collective-permute-start(f32[128,512]{1,0:T(8,128)S(1)} %convolution_select_fusion.2), channel_id=1, source_target_pairs={{32,0},{36,4},{40,8},{44,12},{48,16},{52,20},{56,24},{60,28},{64,3... | collective-permute-start | bytes 786440 | tf_op jit(solution)/shard_map/ppermute | solution.py:31
  328.3 20.6 %collective-permute-start.25 = (f32[128,512]{1,0:T(8,128)S(1)}, f32[128,512]{1,0:T(8,128)S(1)}, u32[]{:S(2)}, u32[]{:S(2)}) collective-permute-start(f32[128,512]{1,0:T(8,128)S(1)} %collective-permute-done.24), channel_id=1, source_target_pairs={{0,1},{1,2},{2,3},{3,0},{4,5},{5,6},{6,7},{7,4},{8,9},{9,10},{10,1... | collective-permute-start | bytes 786440 | tf_op jit(solution)/shard_map/ppermute | solution.py:16
  328.6 6.5 collective-permute-start.18
  331.8 18.4 %collective-permute-start.26 = (f32[128,512]{1,0:T(8,128)S(1)}, f32[128,512]{1,0:T(8,128)S(1)}, u32[]{:S(2)}, u32[]{:S(2)}) collective-permute-start(f32[128,512]{1,0:T(8,128)S(1)} %collective-permute-done.24), channel_id=1, source_target_pairs={{0,3},{1,0},{2,1},{3,2},{4,7},{5,4},{6,5},{7,6},{8,11},{9,8},{10,9... | collective-permute-start | bytes 786440 | tf_op jit(solution)/shard_map/ppermute | solution.py:21
  345.6 14.8 %collective-permute-start.52 = (f32[128,512]{1,0:T(8,128)}, f32[128,512]{1,0:T(8,128)S(1)}, u32[]{:S(2)}, u32[]{:S(2)}) collective-permute-start(f32[128,512]{1,0:T(8,128)} %collective-permute-done.51), channel_id=1, source_target_pairs={{0,1},{1,2},{2,3},{3,0},{4,5},{5,6},{6,7},{7,4},{8,9},{9,10},{10,1... | collective-permute-start | bytes 786440 | tf_op jit(solution)/shard_map/ppermute | solution.py:16
  348.0 13.2 %collective-permute-start.53 = (f32[128,512]{1,0:T(8,128)}, f32[128,512]{1,0:T(8,128)S(1)}, u32[]{:S(2)}, u32[]{:S(2)}) collective-permute-start(f32[128,512]{1,0:T(8,128)} %collective-permute-done.51), channel_id=1, source_target_pairs={{0,3},{1,0},{2,1},{3,2},{4,7},{5,4},{6,5},{7,6},{8,11},{9,8},{10,9... | collective-permute-start | bytes 786440 | tf_op jit(solution)/shard_map/ppermute | solution.py:21
  348.9 7.6 %collective-permute-start.27 = (f32[128,512]{1,0:T(8,128)S(1)}, f32[128,512]{1,0:T(8,128)S(1)}, u32[]{:S(2)}, u32[]{:S(2)}) collective-permute-start(f32[128,512]{1,0:T(8,128)S(1)} %collective-permute-done.25), channel_id=1, source_target_pairs={{0,1},{1,2},{2,3},{3,0},{4,5},{5,6},{6,7},{7,4},{8,9},{9,10},{10,1... | collective-permute-start | bytes 786440 | tf_op jit(solution)/shard_map/ppermute | solution.py:16
  357.2 6.0 collective-permute-start.28
  360.4 12.3 %collective-permute-start.54 = (f32[128,512]{1,0:T(8,128)S(1)}, f32[128,512]{1,0:T(8,128)S(1)}, u32[]{:S(2)}, u32[]{:S(2)}) collective-permute-start(f32[128,512]{1,0:T(8,128)S(1)} %collective-permute-done.52), channel_id=1, source_target_pairs={{0,1},{1,2},{2,3},{3,0},{4,5},{5,6},{6,7},{7,4},{8,9},{9,10},{10,1... | collective-permute-start | bytes 786440 | tf_op jit(solution)/shard_map/ppermute | solution.py:16
  363.2 20.1 %collective-permute-start.29 = (f32[128,512]{1,0:T(8,128)S(1)}, f32[128,512]{1,0:T(8,128)S(1)}, u32[]{:S(2)}, u32[]{:S(2)}) collective-permute-start(f32[128,512]{1,0:T(8,128)S(1)} %collective-permute-done.28), channel_id=1, source_target_pairs={{0,1},{1,2},{2,3},{3,0},{4,5},{5,6},{6,7},{7,4},{8,9},{9,10},{10,1... | collective-permute-start | bytes 786440 | tf_op jit(solution)/shard_map/ppermute | solution.py:16
  364.0 8.7 %collective-permute-start.23 = (f32[4,128]{1,0:T(4,128)S(1)}, f32[4,128]{1,0:T(4,128)S(1)}, u32[]{:S(2)}, u32[]{:S(2)}) collective-permute-start(f32[4,128]{1,0:T(4,128)S(1)} %fusion.30), channel_id=1, source_target_pairs={{0,128},{4,132},{8,136},{12,140},{16,144},{20,148},{24,152},{28,15... | collective-permute-start | bytes 6152 | tf_op jit(solution)/shard_map/ppermute | solution.py:31
  370.0 16.0 %collective-permute-start.30 = (f32[128,512]{1,0:T(8,128)S(1)}, f32[128,512]{1,0:T(8,128)S(1)}, u32[]{:S(2)}, u32[]{:S(2)}) collective-permute-start(f32[128,512]{1,0:T(8,128)S(1)} %collective-permute-done.28), channel_id=1, source_target_pairs={{0,3},{1,0},{2,1},{3,2},{4,7},{5,4},{6,5},{7,6},{8,11},{9,8},{10,9... | collective-permute-start | bytes 786440 | tf_op jit(solution)/shard_map/ppermute | solution.py:21
  383.3 7.8 %collective-permute-start.31 = (f32[128,512]{1,0:T(8,128)S(1)}, f32[128,512]{1,0:T(8,128)S(1)}, u32[]{:S(2)}, u32[]{:S(2)}) collective-permute-start(f32[128,512]{1,0:T(8,128)S(1)} %collective-permute-done.29), channel_id=1, source_target_pairs={{0,1},{1,2},{2,3},{3,0},{4,5},{5,6},{6,7},{7,4},{8,9},{9,10},{10,1... | collective-permute-start | bytes 786440 | tf_op jit(solution)/shard_map/ppermute | solution.py:16
  393.0 8.4 %all-to-all-start = ((f32[4,1,128]{2,1,0:T(1,128)}), f32[4,1,128]{2,1,0:T(1,128)S(1)}, u32[]{:S(2)}, u32[]{:S(2)}) async-start(f32[4,1,128]{2,1,0:T(1,128)} %bitcast.18), calls=%async_computation | async-start | bytes 4096 | tf_op jit(solution)/shard_map/all_to_all | solution.py:121
  397.0 110.3 %collective-permute-start.56 = (f32[128,512]{1,0:T(8,128)S(1)}, f32[128,512]{1,0:T(8,128)S(1)}, u32[]{:S(2)}, u32[]{:S(2)}) collective-permute-start(f32[128,512]{1,0:T(8,128)S(1)} %convolution_select_fusion.1), channel_id=1, source_target_pairs={{64,0},{68,4},{72,8},{76,12},{80,16},{84,20},{88,24},{92,28},{96,3... | collective-permute-start | bytes 786440 | tf_op jit(solution)/shard_map/ppermute | solution.py:31
  498.3 3.2 collective-permute-start.32
  501.5 9.1 %collective-permute-start.33 = (f32[4,128]{1,0:T(4,128)S(1)}, f32[4,128]{1,0:T(4,128)S(1)}, u32[]{:S(2)}, u32[]{:S(2)}) collective-permute-start(f32[4,128]{1,0:T(4,128)S(1)} %broadcast_select_fusion.2), channel_id=1, source_target_pairs={{4,0},{8,4},{12,8},{16,12},{20,16},{24,20},{28,24},{32,28},{36,32}... | collective-permute-start | bytes 6152 | tf_op jit(solution)/shard_map/ppermute | solution.py:31
  507.3 16.3 %collective-permute-start.57 = (f32[128,512]{1,0:T(8,128)S(1)}, f32[128,512]{1,0:T(8,128)S(1)}, u32[]{:S(2)}, u32[]{:S(2)}) collective-permute-start(f32[128,512]{1,0:T(8,128)S(1)} %collective-permute-done.56), channel_id=1, source_target_pairs={{0,1},{1,2},{2,3},{3,0},{4,5},{5,6},{6,7},{7,4},{8,9},{9,10},{10,1... | collective-permute-start | bytes 786440 | tf_op jit(solution)/shard_map/ppermute | solution.py:16
  507.9 50.5 %collective-permute-start.58 = (f32[128,512]{1,0:T(8,128)S(1)}, f32[128,512]{1,0:T(8,128)S(1)}, u32[]{:S(2)}, u32[]{:S(2)}) collective-permute-start(f32[128,512]{1,0:T(8,128)S(1)} %collective-permute-done.56), channel_id=1, source_target_pairs={{0,3},{1,0},{2,1},{3,2},{4,7},{5,4},{6,5},{7,6},{8,11},{9,8},{10,9... | collective-permute-start | bytes 786440 | tf_op jit(solution)/shard_map/ppermute | solution.py:21
  521.4 5.5 collective-permute-start.35
  523.5 53.6 %collective-permute-start.59 = (f32[128,512]{1,0:T(8,128)S(1)}, f32[128,512]{1,0:T(8,128)S(1)}, u32[]{:S(2)}, u32[]{:S(2)}) collective-permute-start(f32[128,512]{1,0:T(8,128)S(1)} %collective-permute-done.57), channel_id=1, source_target_pairs={{0,1},{1,2},{2,3},{3,0},{4,5},{5,6},{6,7},{7,4},{8,9},{9,10},{10,1... | collective-permute-start | bytes 786440 | tf_op jit(solution)/shard_map/ppermute | solution.py:16
  537.8 6.4 collective-permute-start.40
  555.1 9.5 %collective-permute-start.45 = (f32[4,128]{1,0:T(4,128)S(1)}, f32[4,128]{1,0:T(4,128)S(1)}, u32[]{:S(2)}, u32[]{:S(2)}) collective-permute-start(f32[4,128]{1,0:T(4,128)S(1)} %fusion.25), channel_id=1, source_target_pairs={{32,0},{36,4},{40,8},{44,12},{48,16},{52,20},{56,24},{60,28},{64,3... | collective-permute-start | bytes 6152 | tf_op jit(solution)/shard_map/ppermute | solution.py:31
  575.2 5.5 collective-permute-start.50
  591.5 7.1 %collective-permute-start.55 = (f32[4,128]{1,0:T(4,128)S(1)}, f32[4,128]{1,0:T(4,128)S(1)}, u32[]{:S(2)}, u32[]{:S(2)}) collective-permute-start(f32[4,128]{1,0:T(4,128)S(1)} %fusion.23), channel_id=1, source_target_pairs={{128,0},{132,4},{136,8},{140,12},{144,16},{148,20},{152,24},{156,2... | collective-permute-start | bytes 6152 | tf_op jit(solution)/shard_map/ppermute | solution.py:31
  (6 other events, 4.3 us)
Sparse Core Ops, SparseCore 0:
  9.8 29.4 all-gather.1
